TPU v7x, 256 devices: a whole 4x4x8 slice. The times are simulated.
256 devices in a mesh: req: 64 (over z_hi, x, y, core), tp: 4 (over z_lo).
Axes of the slice: x: 4, y: 4, z: 8 (z_hi: 2, z_lo: 4; z = z_hi * 4 + z_lo), core: 2. Of those that a mesh axis runs over, the one named last changes fastest.
Arguments:
- layer_in: bfloat16 [8192, 2048], P('req'), may hold values from -15 to 15
- q_nope: bfloat16 [8192, 2048], P('req', 'tp'), may hold values from -6 to 6
- q_pe: bfloat16 [8192, 1024], P('req', 'tp'), may hold values from -100 to 100
- kv_cache: bfloat16 [128, 1024, 576], P('req'), may hold values from -6 to 6
- lengths: int32 [128], P('req'), may hold values from 2 to 1024, as said below
- parents: int32 [128, 64], P('req'), may hold values from 0 to 62, as said below
- accepted: int32 [128], P('req'), may hold values from 0 to 63
- kv_a: bfloat16 [2048, 576], P(None, 'tp'), may hold values from -0.125 to 0.125
- kv_gain: float32 [512], replicated, may hold values from 0.1 to 1.9
- w_uk: bfloat16 [2048, 512], P('tp'), may hold values from -0.5 to 0.5
- w_uv: bfloat16 [512, 2048], P(None, 'tp'), may hold values from -0.25 to 0.25
- o_proj: bfloat16 [2048, 2048], P('tp'), may hold values from -0.125 to 0.125
- post_gain: float32 [2048], replicated, may hold values from 0.1 to 1.9
- routes: int32 [8192, 6], P('req'), may hold values from 0 to 63, all different within a row; in each aligned block of 128 rows (0 to 127, 128 to 255, ...) at most 16 rows name the same one
- gates: bfloat16 [8192, 6], P('req'), may hold values from 0.14941406 to 0.59765625
- w_gate: bfloat16 [64, 2048, 1408], P('req', None, 'tp'), may hold values from -0.125 to 0.125
- w_up: bfloat16 [64, 2048, 1408], P('req', None, 'tp'), may hold values from -0.125 to 0.125
- w_down: bfloat16 [64, 1408, 2048], P('req', 'tp'), may hold values from -0.15625 to 0.15625
Outputs:
- layer_out: bfloat16 [8192, 2048], P('req', 'tp')
- accepted_rows: bfloat16 [128, 64, 576], P('req')
Inputs may be any that keep to these rules, and one draw needn't show every extreme that they name: `lengths`: at least one request of every draw has 1024 live slots. parents[r, 0] = 0; for i >= 1, parents[r, i] lies from i - 4 to i - 1. `routes`: the 6 experts of a token differ; within each aligned block of 128 rows (the tokens of one device) no expert is named more than 16 times.
All inputs are finite; a program needn't handle non-finite values.
Results may differ from a plain program's by a relative error of at most 0.012.
Values may be sent and summed in bfloat16 or wider, within the bound.
No kernel may reach another device: no remote copies, remote signals or barrier semaphores. Data moves between devices by JAX's collectives and lax.ppermute only.
A program may use at most 128 MiB of HBM per device.

v0:
```python
import jax
import jax.numpy as jnp
from jax import lax
from jax.sharding import PartitionSpec as P

D = 2048
NOPE = 128
ROPE = 64
VDIM = 128
LATENT = 512


epsilon = 1e-06


def ancestors(parent_row):
    tree_size = parent_row.shape[0]
    indices = jnp.arange(tree_size, dtype=jnp.int32)
    link = (
        (parent_row[:, None] == indices[None, :]) | (indices[:, None] == indices[None, :])
    ).astype(jnp.float32)
    for repeat_index in range(tree_size.bit_length()):
        link = jnp.minimum(jnp.dot(link, link, precision=lax.Precision.HIGHEST), 1.0)
    return link


def rotate(vector, positions):
    half_width = vector.shape[-1] // 2
    frequency = 10000.0 ** (-jnp.arange(half_width, dtype=jnp.float32) / half_width)
    angles = positions[:, None] * frequency[None, :]
    first_half = vector[:, :half_width]
    second_half = vector[:, half_width:]
    return jnp.concatenate(
        [
            first_half * jnp.cos(angles) - second_half * jnp.sin(angles),
            first_half * jnp.sin(angles) + second_half * jnp.cos(angles),
        ],
        -1,
    )


def make_rows(compressed, kv_gain, positions):
    latent_raw = compressed[:, :LATENT].astype(jnp.float32)
    new_latent = (
        latent_raw
        * lax.rsqrt(jnp.mean(latent_raw * latent_raw, -1, keepdims=True) + epsilon)
        * kv_gain
    ).astype(jnp.bfloat16)
    new_rotary = rotate(compressed[:, LATENT:].astype(jnp.float32), positions).astype(jnp.bfloat16)
    return jnp.concatenate([new_latent, new_rotary], -1)


def compact(ancestry, depths, node_index, row_set):
    tree_size = ancestry.shape[0]
    chain_mask = jnp.take(ancestry, node_index, axis=0)
    selector = (depths[None, :] == jnp.arange(tree_size, dtype=jnp.float32)[:, None]).astype(
        jnp.float32
    ) * chain_mask[None, :]
    return jnp.dot(
        selector.astype(jnp.bfloat16), row_set, preferred_element_type=jnp.float32
    ).astype(jnp.bfloat16)


def attend_request(q_rows, cache_r, length, new_r, mask_rows):
    score_scale = (NOPE + ROPE) ** (-0.5)
    cache_slots = cache_r.shape[0]
    block_size = min(cache_slots, 512)
    block_total = cache_slots // block_size
    offsets = jnp.arange(block_size, dtype=jnp.int32)
    tree_scores = jnp.dot(q_rows, new_r.T, preferred_element_type=jnp.float32) * score_scale
    tree_scores = jnp.where(mask_rows, tree_scores, -jnp.inf)

    def block_scores(block_index):
        key_block = lax.dynamic_slice_in_dim(cache_r, block_index * block_size, block_size, 0)
        scores = jnp.dot(q_rows, key_block.T, preferred_element_type=jnp.float32) * score_scale
        valid = block_index * block_size + offsets < length
        return (jnp.where(valid[None, :], scores, -jnp.inf), key_block)

    def raise_max(block_index, row_max):
        scores, key_block = block_scores(block_index)
        return jnp.maximum(row_max, jnp.max(scores, -1))

    row_max = lax.fori_loop(0, block_total, raise_max, jnp.max(tree_scores, -1))
    tree_exps = jnp.exp(tree_scores - row_max[:, None])
    start_totals = jnp.sum(tree_exps, -1)
    start_sums = jnp.dot(
        tree_exps.astype(jnp.bfloat16), new_r[:, :LATENT], preferred_element_type=jnp.float32
    )

    def accumulate(block_index, carry):
        totals, weighted = carry
        scores, key_block = block_scores(block_index)
        exps = jnp.exp(scores - row_max[:, None])
        weighted = weighted + jnp.dot(
            exps.astype(jnp.bfloat16), key_block[:, :LATENT], preferred_element_type=jnp.float32
        )
        return (totals + jnp.sum(exps, -1), weighted)

    totals, weighted = lax.fori_loop(0, block_total, accumulate, (start_totals, start_sums))
    return (weighted / totals[:, None]).astype(jnp.bfloat16)


def route_tables(routes, gates, experts_all, capacity):
    tok_rows, top_count = routes.shape
    flat_ids = routes.reshape(-1)
    pair_count = flat_ids.shape[0]
    hit_table = (flat_ids[:, None] == jnp.arange(experts_all, dtype=jnp.int32)[None, :]).astype(
        jnp.bfloat16
    )
    earlier = (
        jnp.arange(pair_count, dtype=jnp.int32)[:, None]
        > jnp.arange(pair_count, dtype=jnp.int32)[None, :]
    ).astype(jnp.bfloat16)
    before = jnp.dot(earlier, hit_table, preferred_element_type=jnp.float32)
    slot_rank = jnp.sum(before * hit_table.astype(jnp.float32), -1).astype(jnp.int32)
    slot_index = flat_ids * capacity + slot_rank
    places = (
        slot_index[:, None] == jnp.arange(experts_all * capacity, dtype=jnp.int32)[None, :]
    ).reshape(tok_rows, top_count, -1)
    pick_table = jnp.any(places, 1).astype(jnp.bfloat16)
    weights = jnp.sum(jnp.where(places, gates[:, :, None], jnp.zeros((), jnp.bfloat16)), 1)
    return (pick_table, weights)


def run_expert(row_set, w_gate, w_up, w_down):
    local_experts = w_gate.shape[0]
    sources = row_set.shape[0] // local_experts
    grouped = row_set.reshape(sources, local_experts, row_set.shape[1], row_set.shape[2])
    gate_act = jnp.einsum("secd,edf->secf", grouped, w_gate, preferred_element_type=jnp.float32)
    up_act = jnp.einsum("secd,edf->secf", grouped, w_up, preferred_element_type=jnp.float32)
    hidden = (jax.nn.silu(gate_act) * up_act).astype(jnp.bfloat16)
    partial_value = jnp.einsum("secf,efd->secd", hidden, w_down, preferred_element_type=jnp.float32)
    return partial_value.reshape(sources * local_experts, row_set.shape[1], -1)


def on_device(
    layer_in,
    q_nope,
    q_pe,
    kv_cache,
    lengths,
    parents,
    accepted,
    kv_a,
    kv_gain,
    w_uk,
    w_uv,
    o_proj,
    post_gain,
    routes,
    gates,
    w_gate,
    w_up,
    w_down,
):
    tok_rows = layer_in.shape[0]
    local_requests, tree_size = parents.shape
    local_heads = q_nope.shape[1] // NOPE
    compressed_part = jnp.dot(layer_in, kv_a, preferred_element_type=jnp.float32).astype(
        jnp.bfloat16
    )
    compressed = lax.all_gather(compressed_part, "tp", axis=1, tiled=True)
    ancestry = jax.vmap(ancestors)(parents)
    depths = jnp.sum(ancestry, -1) - 1.0
    positions = (lengths.astype(jnp.float32)[:, None] + depths).reshape(-1)
    new_rows = make_rows(compressed, kv_gain, positions)
    rows_by_request = new_rows.reshape(local_requests, tree_size, -1)
    accepted_rows = jax.vmap(compact)(ancestry, depths, accepted, rows_by_request)
    query_latent = jnp.einsum(
        "thn,hnl->thl",
        q_nope.reshape(tok_rows, local_heads, NOPE),
        w_uk.reshape(local_heads, NOPE, LATENT),
        preferred_element_type=jnp.float32,
    ).astype(jnp.bfloat16)
    queries = jnp.concatenate([query_latent, q_pe.reshape(tok_rows, local_heads, ROPE)], -1)
    outputs = []
    for request in range(local_requests):
        q_rows = queries[request * tree_size : (request + 1) * tree_size].reshape(
            tree_size * local_heads, -1
        )
        mask_rows = jnp.repeat(ancestry[request] > 0, local_heads, axis=0)
        result = attend_request(
            q_rows, kv_cache[request], lengths[request], rows_by_request[request], mask_rows
        )
        outputs.append(result.reshape(tree_size, local_heads, LATENT))
    latent_out = jnp.concatenate(outputs, 0)
    head_out = jnp.einsum(
        "thl,lhv->thv",
        latent_out,
        w_uv.reshape(LATENT, local_heads, VDIM),
        preferred_element_type=jnp.float32,
    ).astype(jnp.bfloat16)
    attention = jnp.dot(
        head_out.reshape(tok_rows, local_heads * VDIM), o_proj, preferred_element_type=jnp.float32
    )
    experts_all = w_gate.shape[0] * lax.axis_size("req")
    top_count = routes.shape[1]
    capacity = 4 * tok_rows * top_count // (3 * experts_all)
    pick_table, weights = route_tables(routes, gates, experts_all, capacity)
    quarter = D // lax.axis_size("tp")
    tp_index = lax.axis_index("tp")
    residual_sum = layer_in.astype(jnp.float32) + lax.psum(attention, "tp")
    normed = (
        residual_sum
        * lax.rsqrt(jnp.mean(residual_sum * residual_sum, -1, keepdims=True) + epsilon)
        * post_gain
    ).astype(jnp.bfloat16)
    outgoing = lax.dot_general(
        pick_table, normed, (((0,), (0,)), ((), ())), preferred_element_type=jnp.float32
    ).astype(jnp.bfloat16)
    outgoing = outgoing.reshape(experts_all, capacity, D)
    partial_value = run_expert(
        lax.all_to_all(outgoing, "req", split_axis=0, concat_axis=0, tiled=True),
        w_gate,
        w_up,
        w_down,
    )
    returned = lax.all_to_all(partial_value, "req", split_axis=0, concat_axis=0, tiled=True)
    shares = lax.psum_scatter(returned, "tp", scatter_dimension=2, tiled=True).astype(jnp.bfloat16)
    hidden_quarter = lax.dynamic_slice_in_dim(residual_sum, tp_index * quarter, quarter, 1)
    routed = jnp.dot(
        weights, shares.reshape(experts_all * capacity, quarter), preferred_element_type=jnp.float32
    )
    layer_out = (hidden_quarter + routed).astype(jnp.bfloat16)
    return (layer_out, accepted_rows)


def solution(mesh):
    return jax.shard_map(
        on_device,
        mesh=mesh,
        in_specs=(
            P("req", None),
            P("req", "tp"),
            P("req", "tp"),
            P("req", None, None),
            P("req"),
            P("req", None),
            P("req"),
            P(None, "tp"),
            P(),
            P("tp", None),
            P(None, "tp"),
            P("tp", None),
            P(),
            P("req", None),
            P("req", None),
            P("req", None, "tp"),
            P("req", None, "tp"),
            P("req", "tp", None),
        ),
        out_specs=(P("req", "tp"), P("req", None, None)),
        check_vma=False,
    )
```

profile of v0, /device:TPU:1, one launch (start us, length us, event | category | flops | bytes accessed | tf_op | source)
XLA Modules:
  0.0 632.3 jit_solution(311835194629323395)
XLA Ops:
  7.3 1.7 convolution_convert_fusion.4
  9.0 13.4 %all_gather.3 = bf16[128,576]{0,1:T(8,128)(2,1)S(1)} all-gather(bf16[128,144]{0,1:T(8,128)(2,1)S(1)} %convolution_convert_fusion.4), channel_id=1, replica_groups=mesh['req'=64,'tp'=4] {'tp'}, dimensions={1}, use_global_device_ids=true | all-gather | bytes 184320 | tf_op jit(solution)/shard_map/all_gather | solution.py:162
  23.6 0.7 convert_element_type.103
  24.3 1.4 fusion.111
  26.2 1.0 convolution_minimum_fusion.6
  30.1 1.1 slice_maximum_fusion
  31.5 0.9 reshape.205
  33.0 0.7 copy.77
  33.7 3.2 fusion.110
  36.9 1.7 copy.92
  38.6 0.8 fusion.68
  39.5 0.9 fusion.101
  40.4 2.4 fusion.114
  42.8 6.6 %while.60 = (s32[]{:T(128)}, f32[256]{0:T(256)}, s32[]{:T(128)}, bf16[1024,576]{1,0:T(8,128)(2,1)S(1)}, bf16[256,576]{1,0:T(8,128)(2,1)}, /*index=5*/s32[]{:T(128)}, s32[]{:T(128)}, s32[]{:T(128)}, s32[]{:T(128)}) while((s32[]{:T(128)}, f32[256]{0:T(256)}, s32[]{:T(128)}, bf16[1024,576]{1,0:T(8,128)(2,1)S(1)}, ...), condition=%wide.region_5.6_spmd.clone, body=%wide.region_3.5_spmd.clone.sunk | while | flops 151389184 | bytes 955543 | solution.py:83
  42.8 0.7 fusion.169
  43.5 1.4 fusion.170
  44.9 1.2 max.18
  46.1 0.7 fusion.169
  46.8 1.4 fusion.170
  48.2 1.2 max.18
  49.5 1.1 copy-done.1
  50.5 1.2 fusion.76
  51.8 0.9 fusion.82
  52.6 1.3 copy.79
  54.3 2.4 copy.93
  57.1 4.6 while.62
  57.1 0.7 fusion.178
  57.8 1.6 fusion.179
  59.4 0.6 fusion.178
  60.1 1.6 fusion.179
  62.6 7.4 %while.61 = (s32[]{:T(128)}, f32[256]{0:T(256)S(1)}, f32[256,512]{1,0:T(8,128)S(1)}, s32[]{:T(128)}, bf16[1024,576]{1,0:T(8,128)(2,1)}, /*index=5*/bf16[256,576]...) while((s32[]{:T(128)}, f32[256]{0:T(256)S(1)}, ...), condition=%wide.region_9.10_spmd.clone, body=%wide.region_7.9_spmd.clone.sunk | while | flops 286000128 | bytes 3086507 | solution.py:99
  62.6 0.7 fusion.174
  63.3 1.6 fusion.175
  64.9 1.4 convolution_add_fusion.5
  66.4 0.7 fusion.174
  67.0 1.6 fusion.175
  68.7 1.4 convolution_add_fusion.5
  70.6 0.7 divide_convert_fusion.1
  71.4 0.8 copy.82
  72.2 8.5 %while.63 = (s32[]{:T(128)}, f32[256]{0:T(256)}, f32[256,512]{1,0:T(8,128)S(1)}, s32[]{:T(128)}, bf16[1024,576]{1,0:T(8,128)(2,1)}, /*index=5*/bf16[256,576]{1,0...) while((s32[]{:T(128)}, f32[256]{0:T(256)}, ...), condition=%wide.region_17.18_spmd.clone, body=%wide.region_15.17_spmd.clone.sunk | while | flops 286000128 | bytes 3094755 | solution.py:99
  72.9 1.6 fusion.184
  74.5 1.4 convolution_add_fusion.6
  77.1 1.6 fusion.184
  78.8 1.4 convolution_add_fusion.6
  80.7 0.8 divide_convert_fusion
  81.6 1.3 copy.91
  82.9 1.2 convolution_convert_fusion.3
  84.2 1.5 fusion.115
  87.2 65.9 %all-reduce.2.cloned.1.call-done = f32[128,2048]{1,0:T(8,128)} async-done(((f32[128,2048]{1,0:T(8,128)}), f32[128,2048]{1,0:T(8,128)}) %all-reduce.2.cloned.1.call-update) | async-done | bytes 1048592 | tf_op jit(solution)/shard_map/psum | solution.py:202
  153.0 1.6 multiply_reduce_fusion
  154.6 1.3 convolution_convert_fusion
  156.0 109.4 %all_to_all.10 = bf16[64,16,2048]{2,1,0:T(8,128)(2,1)S(1)} all-to-all(bf16[64,16,2048]{2,1,0:T(8,128)(2,1)S(1)} %bitcast.131), channel_id=1, replica_groups=mesh['req'=64,'tp'=4] {'req'}, dimensions={0} | all-to-all | bytes 8388608 | tf_op jit(solution)/shard_map/all_to_all | solution.py:213
  265.4 1.9 copy-done.2
  267.3 3.5 fusion.47
  270.8 11.2 %fusion.44 = f32[64,16,2048]{2,1,0:T(8,128)} fusion(bf16[1,352,2048]{2,1,0:T(8,128)(2,1)} %param.43, bf16[64,16,2048]{2,1,0:T(8,128)(2,1)} %copy-done.2, bf16[1,2048,352]{1,2,0:T(8,128)(2,1)} %param.42, f32[64,16,352]{2,1,0:T(8,128)} %fusion.47), kind=kOutput, calls=%fused_computation.57 | convolution fusion | flops 2954952704 | bytes 16908288 | tf_op jit(solution)/shard_map/secf,efd->secd/dot_general | solution.py:132
  282.0 195.5 %all_to_all.11 = f32[64,16,2048]{2,1,0:T(8,128)} all-to-all(f32[64,16,2048]{2,1,0:T(8,128)} %fusion.44), channel_id=1, replica_groups=mesh['req'=64,'tp'=4] {'req'}, dimensions={0} | all-to-all | bytes 16777216 | tf_op jit(solution)/shard_map/all_to_all | solution.py:218
  477.6 0.8 copy.87
  478.4 1.4 gather_fusion
  479.8 1.2 fusion.39
  481.0 0.7 compare_and_fusion
  481.7 1.8 convolution_convert_fusion.2
  483.5 139.2 %reduce-scatter.2.cloned.1.call-done = f32[64,16,512]{2,1,0:T(8,128)} async-done(((f32[64,16,2048]{2,1,0:T(8,128)}), f32[64,16,512]{2,1,0:T(8,128)}) %reduce-scatter.2.cloned.1.call-update) | async-done | bytes 2097168 | tf_op jit(solution)/shard_map/reduce_scatter | solution.py:219
  622.7 1.7 convert_element_type.117
  624.5 1.0 fusion.56
  (95 shorter events, 11.9 us)
Async XLA Ops:
  7.2 77.0 %copy-start = (bf16[512,2048]{1,0:T(8,128)(2,1)S(1)}, bf16[512,2048]{1,0:T(8,128)(2,1)}, u32[]{:S(2)}) copy-start(bf16[512,2048]{1,0:T(8,128)(2,1)} %param.37) | copy-start | bytes 6291460
  7.2 22.4 %copy-start.11 = (bf16[128,256]{1,0:T(8,128)(2,1)S(1)}, bf16[128,256]{1,0:T(8,128)(2,1)}, u32[]{:S(2)}) copy-start(bf16[128,256]{1,0:T(8,128)(2,1)} %param.28) | copy-start | bytes 196612
  7.2 22.6 %copy-start.6 = (bf16[512,512]{1,0:T(8,128)(2,1)S(1)}, bf16[512,512]{1,0:T(8,128)(2,1)}, u32[]{:S(2)}) copy-start(bf16[512,512]{1,0:T(8,128)(2,1)} %param.35) | copy-start | bytes 1572868
  7.2 22.6 %copy-start.8 = (bf16[128,512]{1,0:T(8,128)(2,1)S(1)}, bf16[128,512]{1,0:T(8,128)(2,1)}, u32[]{:S(2)}) copy-start(bf16[128,512]{1,0:T(8,128)(2,1)} %param.27) | copy-start | bytes 393220
  7.2 145.8 %all-reduce.2.cloned.1.call-start = ((), (), s32[]{:S(2)}) async-start(), calls=%async_computation.3 | async-start | bytes 2097152 | tf_op jit(solution)/shard_map/psum | solution.py:202
  28.4 3.9 copy-start.7
  39.4 1.0 copy-start.3
  49.5 1.1 copy-start.1
  50.5 3.6 copy-start.16
  54.1 2.9 copy-start.5
  57.1 4.6 copy-start.4
  57.1 5.6 copy-start.10
  61.7 0.9 copy-start.9
  70.1 0.5 copy-start.12
  72.8 3.0 copy-start.13
  75.9 0.6 copy-start.14
  77.1 3.0 copy-start.13
  80.2 0.6 copy-start.14
  84.2 1.6 copy-start.17
  85.7 537.0 %reduce-scatter.2.cloned.1.call-start = ((), (), s32[]{:S(2)}) async-start(), calls=%async_computation.4 | async-start | bytes 10485760 | tf_op jit(solution)/shard_map/reduce_scatter | solution.py:219
  86.4 68.2 %copy-start.18 = (f32[2048]{0:T(1024)S(1)}, f32[2048]{0:T(1024)}, u32[]{:S(2)}) copy-start(f32[2048]{0:T(1024)} %param.38) | copy-start | bytes 24580
  86.6 69.3 %copy-start.15 = (s32[128,6]{0,1:T(8,128)}, s32[128,6]{0,1:T(8,128)S(1)}, u32[]{:S(2)}) copy-start(s32[128,6]{0,1:T(8,128)S(1)} %multiply_add_fusion) | copy-start | bytes 9220
  156.0 111.3 %copy-start.19 = (bf16[1,2048,352]{1,2,0:T(8,128)(2,1)S(1)}, bf16[1,2048,352]{1,2,0:T(8,128)(2,1)}, u32[]{:S(2)}) copy-start(bf16[1,2048,352]{1,2,0:T(8,128)(2,1)} %param.41) | copy-start | bytes 4325380
  265.4 1.9 copy-start.2
  477.6 0.8 copy-start.20
Sparse Core Ops, SparseCore 0:
  85.8 67.1 all-reduce.1
  477.7 144.9 reduce-scatter.1
where the time goes:
time: 634 us; the launch traced here: 632 us
  blocking collectives  318 us (50%)
  waiting for transfers between devices  205 us (32%)
  matrix products  48.5 us (8%)
  other arithmetic  22.9 us (4%)
  local copies, waits for them, and re-layouts  22.6 us (4%)
  between operations  14.5 us (2%)
    all_to_all x1, blocking collectives, on_device(): lax.all_to_all(partial_value, 'req', split_axis=0, concat_axis=0, tiled=T...  196 us
    reduce_scatter x1, waiting for transfers between devices, on_device(): lax.psum_scatter(returned, 'tp', scatter_dimension=2, tiled=True)  139 us
    all_to_all x1, blocking collectives, on_device(): lax.all_to_all(outgoing, 'req', split_axis=0, concat_axis=0, tiled=True)  109 us
    psum x1, waiting for transfers between devices, on_device(): residual_sum = layer_in.astype(jnp.float32) + lax.psum(attention, 'tp')  65.9 us
    all_gather x1, blocking collectives, on_device(): compressed = lax.all_gather(compressed_part, 'tp', axis=1, tiled=True)  13.4 us
  transfers between devices with their start and end apart: 2, of which 2 were waited for; matrix products, arithmetic and copies ran while one was open for 1% of the time, Pallas kernels for 0%

commit v1 on v0

--- a/solution.py
+++ b/solution.py
@@ -190,38 +190,54 @@
         w_uv.reshape(LATENT, local_heads, VDIM),
         preferred_element_type=jnp.float32,
     ).astype(jnp.bfloat16)
-    attention = jnp.dot(
-        head_out.reshape(tok_rows, local_heads * VDIM), o_proj, preferred_element_type=jnp.float32
-    )
     experts_all = w_gate.shape[0] * lax.axis_size("req")
     top_count = routes.shape[1]
     capacity = 4 * tok_rows * top_count // (3 * experts_all)
     pick_table, weights = route_tables(routes, gates, experts_all, capacity)
-    quarter = D // lax.axis_size("tp")
+    tp_size = lax.axis_size("tp")
     tp_index = lax.axis_index("tp")
-    residual_sum = layer_in.astype(jnp.float32) + lax.psum(attention, "tp")
-    normed = (
-        residual_sum
-        * lax.rsqrt(jnp.mean(residual_sum * residual_sum, -1, keepdims=True) + epsilon)
-        * post_gain
+    quarter = D // tp_size
+    attention_parts = jnp.einsum(
+        "tk,kqf->qtf",
+        head_out.reshape(tok_rows, local_heads * VDIM),
+        o_proj.reshape(o_proj.shape[0], tp_size, quarter),
+        preferred_element_type=jnp.float32,
+    )
+    attention_quarter = lax.psum_scatter(attention_parts, "tp", scatter_dimension=0, tiled=True)
+    attention_quarter = attention_quarter.reshape(tok_rows, quarter)
+    hidden_quarter = lax.dynamic_slice_in_dim(layer_in, tp_index * quarter, quarter, 1)
+    residual_quarter = hidden_quarter.astype(jnp.float32) + attention_quarter
+    square_sum = lax.psum(jnp.sum(residual_quarter * residual_quarter, -1, keepdims=True), "tp")
+    gain_quarter = lax.dynamic_slice_in_dim(post_gain, tp_index * quarter, quarter, 0)
+    normed_quarter = (
+        residual_quarter * lax.rsqrt(square_sum / D + epsilon) * gain_quarter
     ).astype(jnp.bfloat16)
     outgoing = lax.dot_general(
-        pick_table, normed, (((0,), (0,)), ((), ())), preferred_element_type=jnp.float32
-    ).astype(jnp.bfloat16)
-    outgoing = outgoing.reshape(experts_all, capacity, D)
-    partial_value = run_expert(
-        lax.all_to_all(outgoing, "req", split_axis=0, concat_axis=0, tiled=True),
-        w_gate,
-        w_up,
-        w_down,
-    )
-    returned = lax.all_to_all(partial_value, "req", split_axis=0, concat_axis=0, tiled=True)
-    shares = lax.psum_scatter(returned, "tp", scatter_dimension=2, tiled=True).astype(jnp.bfloat16)
-    hidden_quarter = lax.dynamic_slice_in_dim(residual_sum, tp_index * quarter, quarter, 1)
+        pick_table, normed_quarter, (((0,), (0,)), ((), ())), preferred_element_type=jnp.float32
+    ).astype(jnp.bfloat16)
+    outgoing = outgoing.reshape(experts_all, capacity, quarter)
+    arrived = lax.all_to_all(outgoing, "req", split_axis=0, concat_axis=0, tiled=True)
+    row_set = lax.all_gather(arrived, "tp", axis=0, tiled=False)
+    gate_w = w_gate[0].reshape(tp_size, quarter, -1)
+    up_w = w_up[0].reshape(tp_size, quarter, -1)
+    gate_act = jnp.einsum("qscf,qfh->sch", row_set, gate_w, preferred_element_type=jnp.float32)
+    up_act = jnp.einsum("qscf,qfh->sch", row_set, up_w, preferred_element_type=jnp.float32)
+    expert_hidden = (jax.nn.silu(gate_act) * up_act).astype(jnp.bfloat16)
+    partial_value = jnp.einsum(
+        "sch,hqf->qscf",
+        expert_hidden,
+        w_down[0].reshape(w_down.shape[1], tp_size, quarter),
+        preferred_element_type=jnp.float32,
+    )
+    partial_parts = lax.all_to_all(
+        partial_value.astype(jnp.bfloat16), "tp", split_axis=0, concat_axis=0, tiled=True
+    )
+    expert_out = jnp.sum(partial_parts.astype(jnp.float32), 0).astype(jnp.bfloat16)
+    shares = lax.all_to_all(expert_out, "req", split_axis=0, concat_axis=0, tiled=True)
     routed = jnp.dot(
         weights, shares.reshape(experts_all * capacity, quarter), preferred_element_type=jnp.float32
     )
-    layer_out = (hidden_quarter + routed).astype(jnp.bfloat16)
+    layer_out = (residual_quarter + routed).astype(jnp.bfloat16)
     return (layer_out, accepted_rows)
 
 

time: 634 us -> 413 us (0.65)
  blocking collectives: 318 us -> 161 us
  waiting for transfers between devices: 205 us -> 127 us
  starting transfers between devices: 0.08 us -> 14.1 us
  local copies, waits for them, and re-layouts: 22.6 us -> 35 us
  matrix products: 48.5 us -> 39 us
    reduce_scatter x1, waiting for transfers between devices: 139 us -> 34 us  [on_device(): lax.psum_scatter(attention_parts, 'tp', scatter_dimension=0, tiled=True)]
    all_to_all x1, blocking collectives: 196 us -> 95.7 us  [on_device(): lax.all_to_all(partial_value.astype(jnp.bfloat16), 'tp', split_axis=0, co...]
    all_gather x0 -> x1, waiting for transfers between devices: none -> 66.1 us  [on_device(): row_set = lax.all_gather(arrived, 'tp', axis=0, tiled=False)]
    psum x1 -> x0, waiting for transfers between devices: 65.9 us -> none  [on_device(): residual_sum = layer_in.astype(jnp.float32) + lax.psum(attention, 'tp')]
    all_to_all x1, blocking collectives: 109 us -> 44.8 us  [on_device(): lax.all_to_all(outgoing, 'req', split_axis=0, concat_axis=0, tiled=True)]
    all_to_all x0 -> x1, waiting for transfers between devices: none -> 26.5 us  [on_device(): lax.all_to_all(expert_out, 'req', split_axis=0, concat_axis=0, tiled=True)]
    all_to_all x0 -> x1, starting transfers between devices: none -> 14 us  [on_device(): lax.all_to_all(expert_out, 'req', split_axis=0, concat_axis=0, tiled=True)]
    another operation x0 -> x3, local copies, waits for them, and re-layouts: none -> 13.2 us  [the longest x1 4.44 us: on_device(): w_down[0].reshape(w_down.shape[1], tp_size, quarter)]
  transfers between devices with their start and end apart: 2 -> 3, of which waited for: 2 -> 3; matrix products, arithmetic and copies ran while one was open for 1% -> 4% of each run, Pallas kernels for 0% -> 0%
where the time goes in v1:
time: 413 us; the launch traced here: 411 us
  blocking collectives  161 us (39%)
  waiting for transfers between devices  127 us (31%)
  matrix products  39 us (9%)
  local copies, waits for them, and re-layouts  35 us (8%)
  other arithmetic  20.2 us (5%)
  between operations  14.5 us (4%)
  starting transfers between devices  14.1 us (3%)
    all_to_all x1, blocking collectives, on_device(): lax.all_to_all(partial_value.astype(jnp.bfloat16), 'tp', split_axis=0, co...  95.7 us
    all_gather x1, waiting for transfers between devices, on_device(): row_set = lax.all_gather(arrived, 'tp', axis=0, tiled=False)  66.1 us
    all_to_all x1, blocking collectives, on_device(): lax.all_to_all(outgoing, 'req', split_axis=0, concat_axis=0, tiled=True)  44.8 us
    reduce_scatter x1, waiting for transfers between devices, on_device(): lax.psum_scatter(attention_parts, 'tp', scatter_dimension=0, tiled=True)  34 us
    all_to_all x1, waiting for transfers between devices, on_device(): lax.all_to_all(expert_out, 'req', split_axis=0, concat_axis=0, tiled=True)  26.5 us
    all_to_all x1, starting transfers between devices, on_device(): lax.all_to_all(expert_out, 'req', split_axis=0, concat_axis=0, tiled=True)  14 us
    all_gather x1, blocking collectives, on_device(): compressed = lax.all_gather(compressed_part, 'tp', axis=1, tiled=True)  13.4 us
    dot_general x1, matrix products, on_device(): jnp.einsum('sch,hqf->qscf', expert_hidden, w_down[0].reshape(w_down.shape...  10 us
  transfers between devices with their start and end apart: 3, of which 3 were waited for; matrix products, arithmetic and copies ran while one was open for 4% of the time, Pallas kernels for 0%

profile of v1, /device:TPU:1, one launch (start us, length us, event | category | flops | bytes accessed | tf_op | source)
XLA Modules:
  0.0 411.0 jit_solution(1906855906118336451)
XLA Ops:
  7.3 1.0 copy-done
  8.2 1.4 convolution_convert_fusion.4
  9.7 13.4 %all_gather.9 = bf16[128,576]{0,1:T(8,128)(2,1)S(1)} all-gather(bf16[128,144]{0,1:T(8,128)(2,1)S(1)} %convolution_convert_fusion.4), channel_id=1, replica_groups=mesh['req'=64,'tp'=4] {'tp'}, dimensions={1}, use_global_device_ids=true | all-gather | bytes 184320 | tf_op jit(solution)/shard_map/all_gather | solution.py:162
  23.2 0.6 multiply_power_fusion
  23.8 0.6 fusion.118
  24.3 0.6 add_rsqrt_fusion
  26.4 0.6 broadcast_add_fusion
  27.0 0.6 add.256
  28.1 1.0 slice_maximum_fusion
  29.4 0.9 reshape.182
  30.3 0.6 fusion.99
  31.0 2.9 fusion.117
  33.9 0.7 copy.147
  35.0 1.2 fusion.121
  36.2 4.1 while.60
  36.2 0.6 fusion.174
  36.8 1.4 fusion.175
  38.8 1.4 fusion.175
  40.6 0.6 fusion.88
  41.2 1.0 copy.119
  42.1 1.1 reshape.185
  43.4 2.4 copy.148
  46.2 4.3 %while.62 = (s32[]{:T(128)}, f32[256]{0:T(256)S(1)}, s32[]{:T(128)}, bf16[1024,576]{1,0:T(8,128)(2,1)}, bf16[256,576]{1,0:T(8,128)(2,1)S(1)}, /*index=5*/s32[]{:T(128)}, s32[]{:T(128)}, s32[]{:T(128)}, s32[]{:T(128)}) while((s32[]{:T(128)}, f32[256]{0:T(256)S(1)}, s32[]{:T(128)}, bf16[1024,576]{1,0:T(8,128)(2,1)}, ...), condition=%wide.region_13.14_spmd.clone, body=%wide.region_11.13_spmd.clone.sunk | while | flops 151389184 | bytes 955543 | solution.py:83
  46.2 0.6 fusion.183
  46.8 1.5 fusion.184
  48.3 0.6 fusion.183
  48.9 1.5 fusion.184
  50.5 0.7 copy-done.6
  51.5 0.6 fusion.90
  52.1 7.1 %while.61 = (s32[]{:T(128)}, f32[256]{0:T(256)}, f32[256,512]{1,0:T(8,128)S(1)}, s32[]{:T(128)}, bf16[1024,576]{1,0:T(8,128)(2,1)S(1)}, /*index=5*/bf16[256,576]...) while((s32[]{:T(128)}, f32[256]{0:T(256)}, ...), condition=%wide.region_9.10_spmd.clone, body=%wide.region_7.9_spmd.clone.sunk | while | flops 286000128 | bytes 3053739 | solution.py:99
  52.7 1.4 fusion.180
  54.4 1.2 add.366
  56.2 1.4 fusion.180
  58.0 1.2 add.366
  59.2 1.6 divide_convert_fusion.1
  60.8 1.0 reshape.183
  61.9 0.8 copy.122
  62.6 2.8 while.63
  62.6 0.6 fusion.188
  64.0 0.6 fusion.188
  65.6 0.7 copy.123
  66.4 2.0 copy.141
  68.4 1.4 convolution_convert_fusion.3
  69.9 1.5 fusion.52
  72.3 0.8 dynamic_slice.35
  73.5 34.0 %reduce-scatter.2.cloned.1.call-done = f32[1,128,512]{2,1,0:T(8,128)} async-done(((f32[4,128,512]{2,1,0:T(8,128)}), f32[1,128,512]{2,1,0:T(8,128)}) %reduce-scatter.2.cloned.1.call-update) | async-done | bytes 262160 | tf_op jit(solution)/shard_map/reduce_scatter | solution.py:206
  107.5 1.1 multiply_reduce_fusion
  108.6 7.4 %psum.7 = f32[128,1]{0,1:T(1,128)S(1)} all-reduce(f32[128,1]{0,1:T(1,128)S(1)} %bitcast.156), channel_id=1, replica_groups=mesh['req'=64,'tp'=4] {'tp'}, use_global_device_ids=true, to_apply=%region_23.24 | all-reduce | flops 128 | bytes 1024 | tf_op jit(solution)/shard_map/psum | solution.py:210
  116.0 1.5 convolution_convert_fusion
  117.5 44.8 %all_to_all.15 = bf16[64,16,512]{2,1,0:T(8,128)(2,1)} all-to-all(bf16[64,16,512]{2,1,0:T(8,128)(2,1)S(1)} %bitcast.145), channel_id=1, replica_groups=mesh['req'=64,'tp'=4] {'req'}, dimensions={0} | all-to-all | bytes 2097152 | tf_op jit(solution)/shard_map/all_to_all | solution.py:219
  162.3 4.4 %reshape_squeeze.9 = bf16[4,512,352]{1,0,2:T(4,128)(2,1)} reshape(bf16[1,2048,352]{1,2,0:T(8,128)(2,1)} %param.41) | data formatting | bytes 2883584 | tf_op jit(solution)/shard_map/reshape;squeeze | solution.py:221
  166.7 4.4 %reshape_squeeze.10 = bf16[4,512,352]{1,0,2:T(4,128)(2,1)} reshape(bf16[1,2048,352]{1,2,0:T(8,128)(2,1)} %param.42) | data formatting | bytes 2883584 | tf_op jit(solution)/shard_map/reshape;squeeze | solution.py:222
  171.1 4.4 %reshape_squeeze.11 = bf16[352,4,512]{2,1,0:T(4,128)(2,1)} reshape(bf16[1,352,2048]{2,1,0:T(8,128)(2,1)} %param.43) | data formatting | bytes 2883584 | tf_op jit(solution)/shard_map/reshape;squeeze | solution.py:229
  175.5 66.1 %all-gather.3.cloned.1.call-done = bf16[256,16,512]{2,1,0:T(8,128)(2,1)} async-done(((bf16[64,16,512]{2,1,0:T(8,128)(2,1)}), bf16[256,16,512]{2,1,0:T(8,128)(2,1)}) %all-gather.3.cloned.1.call-update) | async-done | bytes 4194320 | tf_op jit(solution)/shard_map/all_gather | solution.py:220
  241.6 6.2 %fusion.49 = f32[64,16,352,1]{2,1,0,3:T(8,128)} fusion(bf16[4,64,16,512]{3,2,1,0:T(8,128)(2,1)} %bitcast.157, bf16[4,512,352,1]{1,0,2,3:T(4,128)(2,1)} %bitcast.148), kind=kOutput, calls=%fused_computation.63 | convolution fusion | flops 1476395008 | bytes 7077888 | tf_op jit(solution)/shard_map/qscf,qfh->sch/dot_general | solution.py:223
  247.8 10.0 %convert_bitcast_fusion = bf16[4,64,16,512]{3,2,0,1:T(8,128)(2,1)} fusion(bf16[352,4,512]{2,1,0:T(4,128)(2,1)} %reshape_squeeze.11, bf16[4,64,16,512]{3,2,1,0:T(8,128)(2,1)} %bitcast.158, bf16[4,512,352,1]{1,0,2,3:T(4,128)(2,1)} %bitcast.147, f32[64,16,352,1]{2,1,0,3:T(8,128)} %fusion.49), kind=kOutput, calls=%fused_computation.43 | convolution fusion | flops 2957049856 | bytes 12713984 | tf_op jit(solution)/shard_map/sch,hqf->qscf/dot_general | solution.py:226
  257.8 2.6 copy.132
  260.5 95.7 %all_to_all.16 = bf16[4,64,16,512]{3,2,1,0:T(8,128)(2,1)} all-to-all(bf16[4,64,16,512]{3,2,1,0:T(8,128)(2,1)S(1)} %copy.132), channel_id=1, replica_groups=mesh['req'=64,'tp'=4] {'tp'}, dimensions={0} | all-to-all | bytes 8388608 | tf_op jit(solution)/shard_map/all_to_all | solution.py:232
  356.1 4.4 %reduce_sum.111 = bf16[64,16,512]{2,1,0:T(8,128)(2,1)} reduce(bf16[4,64,16,512]{3,2,1,0:T(8,128)(2,1)} %all_to_all.16, bf16[]{:T(256)} %constant.227.clone.1), dimensions={0}, to_apply=%region_24.25 | reduce | flops 1572864 | bytes 5242882 | tf_op jit(solution)/shard_map/reduce_sum | solution.py:235
  360.5 14.0 %all-to-all-start.2 = ((bf16[64,16,512]{2,1,0:T(8,128)(2,1)}), bf16[64,16,512]{2,1,0:T(8,128)(2,1)S(1)}, u32[]{:S(2)}, u32[]{:S(2)}) async-start(bf16[64,16,512]{2,1,0:T(8,128)(2,1)} %reduce_sum.111), calls=%async_computation.3 | async-start | bytes 2097152 | tf_op jit(solution)/shard_map/all_to_all | solution.py:236
  374.7 0.6 gather_fusion
  375.8 0.9 convolution_convert_fusion.2
  376.7 26.5 %all-to-all-done.2 = bf16[64,16,512]{2,1,0:T(8,128)(2,1)S(1)} async-done(((bf16[64,16,512]{2,1,0:T(8,128)(2,1)}), bf16[64,16,512]{2,1,0:T(8,128)(2,1)S(1)}, u32[]{:S(2)}, u32[]{:S(2)}) %all-to-all-start.2) | async-done | bytes 1048608 | tf_op jit(solution)/shard_map/all_to_all | solution.py:236
  403.2 1.0 fusion.60
  (109 shorter events, 10.0 us)
Async XLA Ops:
  7.2 1.1 copy-start
  7.2 16.6 %copy-start.20 = (s32[2]{0:T(128)S(1)}, s32[2]{0:T(128)}, u32[]{:S(2)}) copy-start(s32[2]{0:T(128)} %param.30) | copy-start | bytes 28
  7.2 17.7 %copy-start.24 = (s32[2,64]{1,0:T(2,128)S(1)}, s32[2,64]{1,0:T(2,128)}, u32[]{:S(2)}) copy-start(s32[2,64]{1,0:T(2,128)} %param.31) | copy-start | bytes 1540
  7.2 20.4 %copy-start.13 = (bf16[128,256]{1,0:T(8,128)(2,1)S(1)}, bf16[128,256]{1,0:T(8,128)(2,1)}, u32[]{:S(2)}) copy-start(bf16[128,256]{1,0:T(8,128)(2,1)} %param.28) | copy-start | bytes 196612
  7.2 100.3 %reduce-scatter.2.cloned.1.call-start = ((), (), s32[]{:S(2)}) async-start(), calls=%async_computation.4 | async-start | bytes 1310720 | tf_op jit(solution)/shard_map/reduce_scatter | solution.py:206
  8.2 19.4 %copy-start.8 = (bf16[512,512]{1,0:T(8,128)(2,1)S(1)}, bf16[512,512]{1,0:T(8,128)(2,1)}, u32[]{:S(2)}) copy-start(bf16[512,512]{1,0:T(8,128)(2,1)} %param.35) | copy-start | bytes 1572868
  8.2 19.5 %copy-start.10 = (bf16[128,512]{1,0:T(8,128)(2,1)S(1)}, bf16[128,512]{1,0:T(8,128)(2,1)}, u32[]{:S(2)}) copy-start(bf16[128,512]{1,0:T(8,128)(2,1)} %param.27) | copy-start | bytes 393220
  33.9 0.7 copy-start.18
  33.9 0.7 copy-start.22
  33.9 0.9 copy-start.21
  33.9 0.9 copy-start.23
  36.2 5.0 %copy-start.2 = (bf16[64,4,576]{0,2,1:T(8,128)(2,1)S(1)}, bf16[64,4,576]{0,2,1:T(8,128)(2,1)}, u32[]{:S(2)}) copy-start(bf16[64,4,576]{0,2,1:T(8,128)(2,1)} %get-tuple-element.617) | copy-start | bytes 884740
  40.3 3.0 copy-start.15
  50.5 0.7 copy-start.6
  50.5 1.6 copy-start.11
  59.2 3.4 copy-start.1
  59.2 3.4 copy-start.7
  59.2 3.4 copy-start.12
  59.2 3.4 copy-start.14
  65.4 3.0 copy-start.9
  65.6 4.2 %copy-start.4 = (bf16[512,2048]{1,0:T(8,128)(2,1)S(1)}, bf16[512,2048]{1,0:T(8,128)(2,1)}, u32[]{:S(2)}) copy-start(bf16[512,2048]{1,0:T(8,128)(2,1)} %param.37) | copy-start | bytes 6291460
  69.9 1.6 copy-start.16
  71.3 36.2 %copy-start.5 = (bf16[128,2048]{1,0:T(8,128)(2,1)S(1)}, bf16[128,2048]{1,0:T(8,128)(2,1)}, u32[]{:S(2)}) copy-start(bf16[128,2048]{1,0:T(8,128)(2,1)} %param.26) | copy-start | bytes 1572868
  71.4 170.2 %all-gather.3.cloned.1.call-start = ((), (), s32[]{:S(2)}) async-start(), calls=%async_computation.5 | async-start | bytes 5242880 | tf_op jit(solution)/shard_map/all_gather | solution.py:220
  360.5 14.2 %copy-start.25 = (s32[2]{0:T(128)S(1)}, s32[2]{0:T(128)}, u32[]{:S(2)}) copy-start(s32[2]{0:T(128)} %param.32) | copy-start | bytes 28
  360.5 14.8 %copy-start.19 = (bf16[128,6]{0,1:T(8,128)(2,1)S(1)}, bf16[128,6]{0,1:T(8,128)(2,1)}, u32[]{:S(2)}) copy-start(bf16[128,6]{0,1:T(8,128)(2,1)} %param.40) | copy-start | bytes 4612
  360.5 15.3 %copy-start.17 = (f32[2,64]{1,0:T(2,128)S(1)}, f32[2,64]{1,0:T(2,128)}, u32[]{:S(2)}) copy-start(f32[2,64]{1,0:T(2,128)} %get-tuple-element.622) | copy-start | bytes 1540
  360.5 42.6 %copy-start.3 = (f32[1,128,512]{2,1,0:T(8,128)S(1)}, f32[1,128,512]{2,1,0:T(8,128)}, u32[]{:S(2)}) copy-start(f32[1,128,512]{2,1,0:T(8,128)} %reduce-scatter.2.cloned.1.call-done) | copy-start | bytes 786436
  360.5 42.6 %all-to-all-start.2 = ((bf16[64,16,512]{2,1,0:T(8,128)(2,1)}), bf16[64,16,512]{2,1,0:T(8,128)(2,1)S(1)}, u32[]{:S(2)}, u32[]{:S(2)}) async-start(bf16[64,16,512]{2,1,0:T(8,128)(2,1)} %reduce_sum.111), calls=%async_computation.3 | async-start | bytes 2097152 | tf_op jit(solution)/shard_map/all_to_all | solution.py:236
Sparse Core Ops, SparseCore 0:
  71.5 35.9 reduce-scatter.1
  162.4 79.1 all-gather.2

commit v2 on v1

--- a/solution.py
+++ b/solution.py
@@ -98,6 +98,32 @@
 
     totals, weighted = lax.fori_loop(0, block_total, accumulate, (start_totals, start_sums))
     return (weighted / totals[:, None]).astype(jnp.bfloat16)
+
+
+def attend_dense(q_rows, cache, lengths, new_rows, mask_rows):
+    score_scale = (NOPE + ROPE) ** (-0.5)
+    cache_slots = cache.shape[1]
+    cache_scores = (
+        jnp.einsum("rqk,rck->rqc", q_rows, cache, preferred_element_type=jnp.float32) * score_scale
+    )
+    valid = jnp.arange(cache_slots, dtype=jnp.int32)[None, :] < lengths[:, None]
+    cache_scores = jnp.where(valid[:, None, :], cache_scores, -jnp.inf)
+    tree_scores = (
+        jnp.einsum("rqk,ruk->rqu", q_rows, new_rows, preferred_element_type=jnp.float32)
+        * score_scale
+    )
+    tree_scores = jnp.where(mask_rows, tree_scores, -jnp.inf)
+    row_max = jnp.maximum(jnp.max(cache_scores, -1), jnp.max(tree_scores, -1))
+    cache_exps = jnp.exp(cache_scores - row_max[..., None])
+    tree_exps = jnp.exp(tree_scores - row_max[..., None])
+    totals = jnp.sum(cache_exps, -1) + jnp.sum(tree_exps, -1)
+    summed = jnp.einsum(
+        "rqc,rck->rqk", cache_exps.astype(jnp.bfloat16), cache, preferred_element_type=jnp.float32
+    )
+    summed = summed + jnp.einsum(
+        "rqu,ruk->rqk", tree_exps.astype(jnp.bfloat16), new_rows, preferred_element_type=jnp.float32
+    )
+    return (summed[..., :LATENT] / totals[..., None]).astype(jnp.bfloat16)
 
 
 def route_tables(routes, gates, experts_all, capacity):
@@ -173,17 +199,10 @@
         preferred_element_type=jnp.float32,
     ).astype(jnp.bfloat16)
     queries = jnp.concatenate([query_latent, q_pe.reshape(tok_rows, local_heads, ROPE)], -1)
-    outputs = []
-    for request in range(local_requests):
-        q_rows = queries[request * tree_size : (request + 1) * tree_size].reshape(
-            tree_size * local_heads, -1
-        )
-        mask_rows = jnp.repeat(ancestry[request] > 0, local_heads, axis=0)
-        result = attend_request(
-            q_rows, kv_cache[request], lengths[request], rows_by_request[request], mask_rows
-        )
-        outputs.append(result.reshape(tree_size, local_heads, LATENT))
-    latent_out = jnp.concatenate(outputs, 0)
+    q_rows = queries.reshape(local_requests, tree_size * local_heads, -1)
+    mask_rows = jnp.repeat(ancestry > 0, local_heads, axis=1)
+    latent_out = attend_dense(q_rows, kv_cache, lengths, rows_by_request, mask_rows)
+    latent_out = latent_out.reshape(tok_rows, local_heads, LATENT)
     head_out = jnp.einsum(
         "thl,lhv->thv",
         latent_out,

time: 413 us -> 385 us (0.932)
  local copies, waits for them, and re-layouts: 35 us -> 22.3 us
  other arithmetic: 20.2 us -> 9.89 us
    dot_general x16 -> x4, matrix products: 13 us -> 5.07 us  [the longest x1 2.23 us: attend_dense(): jnp.einsum('rqk,rck->rqc', q_rows, cache, preferred_element_type=jnp.floa...]
    unnamed x56 -> x23, local copies, waits for them, and re-layouts: 5.16 us -> 0.17 us
    slice x4 -> x0, local copies, waits for them, and re-layouts: 4.7 us -> none  [the longest x1 2.86 us: on_device(): kv_cache[request]]
  transfers between devices with their start and end apart: 3 -> 3, of which waited for: 3 -> 3; matrix products, arithmetic and copies ran while one was open for 4% -> 5% of each run, Pallas kernels for 0% -> 0%
where the time goes in v2:
time: 385 us; the launch traced here: 383 us
  blocking collectives  161 us (42%)
  waiting for transfers between devices  125 us (32%)
  matrix products  35.6 us (9%)
  local copies, waits for them, and re-layouts  22.3 us (6%)
  between operations  14.4 us (4%)
  starting transfers between devices  14.1 us (4%)
  other arithmetic  9.89 us (3%)
    all_to_all x1, blocking collectives, on_device(): lax.all_to_all(partial_value.astype(jnp.bfloat16), 'tp', split_axis=0, co...  95.7 us
    all_gather x1, waiting for transfers between devices, on_device(): row_set = lax.all_gather(arrived, 'tp', axis=0, tiled=False)  66.1 us
    all_to_all x1, blocking collectives, on_device(): lax.all_to_all(outgoing, 'req', split_axis=0, concat_axis=0, tiled=True)  44.8 us
    reduce_scatter x1, waiting for transfers between devices, on_device(): lax.psum_scatter(attention_parts, 'tp', scatter_dimension=0, tiled=True)  34 us
    all_to_all x1, waiting for transfers between devices, on_device(): lax.all_to_all(expert_out, 'req', split_axis=0, concat_axis=0, tiled=True)  25.1 us
    all_to_all x1, starting transfers between devices, on_device(): lax.all_to_all(expert_out, 'req', split_axis=0, concat_axis=0, tiled=True)  14 us
    all_gather x1, blocking collectives, on_device(): compressed = lax.all_gather(compressed_part, 'tp', axis=1, tiled=True)  13.4 us
    dot_general x1, matrix products, on_device(): jnp.einsum('sch,hqf->qscf', expert_hidden, w_down[0].reshape(w_down.shape...  10 us
  transfers between devices with their start and end apart: 3, of which 3 were waited for; matrix products, arithmetic and copies ran while one was open for 5% of the time, Pallas kernels for 0%

profile of v2, /device:TPU:1, one launch (start us, length us, event | category | flops | bytes accessed | tf_op | source)
XLA Modules:
  0.0 382.7 jit_solution(10563862629169454771)
XLA Ops:
  7.3 1.7 convolution_convert_fusion.4
  9.0 13.4 %all_gather.9 = bf16[128,576]{0,1:T(8,128)(2,1)S(1)} all-gather(bf16[128,144]{0,1:T(8,128)(2,1)S(1)} %convolution_convert_fusion.4), channel_id=1, replica_groups=mesh['req'=64,'tp'=4] {'tp'}, dimensions={1}, use_global_device_ids=true | all-gather | bytes 184320 | tf_op jit(solution)/shard_map/all_gather | solution.py:188
  22.4 0.1 fusion.43
  22.5 0.7 convert_element_type.95
  23.2 0.7 iota_compare_fusion.12
  23.9 1.0 convolution_minimum_fusion.6
  24.9 0.2 convolution_minimum_fusion.5
  25.1 0.2 convolution_minimum_fusion.4
  25.3 0.2 convolution_minimum_fusion.3
  25.5 0.2 convolution_minimum_fusion.2
  25.7 0.2 convolution_minimum_fusion.1
  25.9 0.3 fusion.80
  26.1 0.1 broadcast_add_fusion
  26.2 0.1 add.82
  26.3 0.1 fusion.45
  26.5 0.1 fusion.69
  26.6 0.8 copy.102
  27.5 0.1 broadcast_in_dim.42
  27.5 0.7 copy.103
  28.3 0.3 fusion.25
  28.6 0.4 copy.97
  29.0 0.1 concatenate.14
  29.1 1.0 copy.98
  30.1 0.1 concatenate.15
  30.2 0.1 copy.99
  30.3 1.4 fusion.81
  31.8 2.2 fusion.6
  34.1 0.4 fusion.54
  34.4 0.6 fusion.7
  35.0 1.1 fusion.30
  36.1 0.2 fusion.33
  36.3 0.9 reshape.161
  37.2 0.2 copy.120
  37.5 1.4 convolution_convert_fusion.3
  38.8 3.1 fusion.19
  42.0 0.0 all-gather.3.cloned.1.call-start
  42.1 0.1 copy.108
  42.2 0.1 eq.78
  42.3 0.4 fusion.29
  42.7 0.1 convert_element_type.104
  42.8 0.1 copy.109
  42.9 0.8 dynamic_slice.7
  43.7 0.5 fusion
  44.2 34.0 %reduce-scatter.2.cloned.1.call-done = f32[1,128,512]{2,1,0:T(8,128)} async-done(((f32[4,128,512]{2,1,0:T(8,128)}), f32[1,128,512]{2,1,0:T(8,128)}) %reduce-scatter.2.cloned.1.call-update) | async-done | bytes 262160 | tf_op jit(solution)/shard_map/reduce_scatter | solution.py:225
  78.1 1.1 multiply_reduce_fusion
  79.2 7.4 %psum.7 = f32[128,1]{0,1:T(1,128)S(1)} all-reduce(f32[128,1]{0,1:T(1,128)S(1)} %bitcast.128), channel_id=1, replica_groups=mesh['req'=64,'tp'=4] {'tp'}, use_global_device_ids=true, to_apply=%region_11.12 | all-reduce | flops 128 | bytes 1024 | tf_op jit(solution)/shard_map/psum | solution.py:229
  86.6 1.5 convolution_convert_fusion
  88.1 44.8 %all_to_all.15 = bf16[64,16,512]{2,1,0:T(8,128)(2,1)} all-to-all(bf16[64,16,512]{2,1,0:T(8,128)(2,1)S(1)} %bitcast.117), channel_id=1, replica_groups=mesh['req'=64,'tp'=4] {'req'}, dimensions={0} | all-to-all | bytes 2097152 | tf_op jit(solution)/shard_map/all_to_all | solution.py:238
  132.9 4.4 %reshape_squeeze.9 = bf16[4,512,352]{1,0,2:T(4,128)(2,1)} reshape(bf16[1,2048,352]{1,2,0:T(8,128)(2,1)} %param.33) | data formatting | bytes 2883584 | tf_op jit(solution)/shard_map/reshape;squeeze | solution.py:240
  137.3 4.4 %reshape_squeeze.10 = bf16[4,512,352]{1,0,2:T(4,128)(2,1)} reshape(bf16[1,2048,352]{1,2,0:T(8,128)(2,1)} %param.34) | data formatting | bytes 2883584 | tf_op jit(solution)/shard_map/reshape;squeeze | solution.py:241
  141.7 4.4 %reshape_squeeze.11 = bf16[352,4,512]{2,1,0:T(4,128)(2,1)} reshape(bf16[1,352,2048]{2,1,0:T(8,128)(2,1)} %param.35) | data formatting | bytes 2883584 | tf_op jit(solution)/shard_map/reshape;squeeze | solution.py:248
  146.2 66.1 %all-gather.3.cloned.1.call-done = bf16[256,16,512]{2,1,0:T(8,128)(2,1)} async-done(((bf16[64,16,512]{2,1,0:T(8,128)(2,1)}), bf16[256,16,512]{2,1,0:T(8,128)(2,1)}) %all-gather.3.cloned.1.call-update) | async-done | bytes 4194320 | tf_op jit(solution)/shard_map/all_gather | solution.py:239
  212.2 6.2 %fusion.16 = f32[64,16,352,1]{2,1,0,3:T(8,128)} fusion(bf16[4,64,16,512]{3,2,1,0:T(8,128)(2,1)} %bitcast.129, bf16[4,512,352,1]{1,0,2,3:T(4,128)(2,1)} %bitcast.123), kind=kOutput, calls=%fused_computation.26 | convolution fusion | flops 1476395008 | bytes 7077888 | tf_op jit(solution)/shard_map/qscf,qfh->sch/dot_general | solution.py:242
  218.4 10.0 %convert_bitcast_fusion = bf16[4,64,16,512]{3,2,0,1:T(8,128)(2,1)} fusion(bf16[352,4,512]{2,1,0:T(4,128)(2,1)} %reshape_squeeze.11, bf16[4,64,16,512]{3,2,1,0:T(8,128)(2,1)} %bitcast.130, bf16[4,512,352,1]{1,0,2,3:T(4,128)(2,1)} %bitcast.122, f32[64,16,352,1]{2,1,0,3:T(8,128)} %fusion.16), kind=kOutput, calls=%fused_computation.1 | convolution fusion | flops 2957049856 | bytes 12713984 | tf_op jit(solution)/shard_map/sch,hqf->qscf/dot_general | solution.py:245
  228.4 2.6 copy.113
  231.1 95.7 %all_to_all.16 = bf16[4,64,16,512]{3,2,1,0:T(8,128)(2,1)} all-to-all(bf16[4,64,16,512]{3,2,1,0:T(8,128)(2,1)S(1)} %copy.113), channel_id=1, replica_groups=mesh['req'=64,'tp'=4] {'tp'}, dimensions={0} | all-to-all | bytes 8388608 | tf_op jit(solution)/shard_map/all_to_all | solution.py:251
  326.8 4.4 %reduce_sum.85 = bf16[64,16,512]{2,1,0:T(8,128)(2,1)} reduce(bf16[4,64,16,512]{3,2,1,0:T(8,128)(2,1)} %all_to_all.16, bf16[]{:T(256)} %constant.56.clone.1), dimensions={0}, to_apply=%region_12.13 | reduce | flops 1572864 | bytes 5242882 | tf_op jit(solution)/shard_map/reduce_sum | solution.py:254
  331.2 14.0 %all-to-all-start.2 = ((bf16[64,16,512]{2,1,0:T(8,128)(2,1)}), bf16[64,16,512]{2,1,0:T(8,128)(2,1)S(1)}, u32[]{:S(2)}, u32[]{:S(2)}) async-start(bf16[64,16,512]{2,1,0:T(8,128)(2,1)} %reduce_sum.85), calls=%async_computation.3 | async-start | bytes 2097152 | tf_op jit(solution)/shard_map/all_to_all | solution.py:255
  345.2 0.6 gather_fusion
  345.8 1.1 fusion.9
  346.9 0.1 broadcast_select_fusion
  347.0 1.8 convolution_convert_fusion.2
  348.7 25.1 %all-to-all-done.2 = bf16[64,16,512]{2,1,0:T(8,128)(2,1)S(1)} async-done(((bf16[64,16,512]{2,1,0:T(8,128)(2,1)}), bf16[64,16,512]{2,1,0:T(8,128)(2,1)S(1)}, u32[]{:S(2)}, u32[]{:S(2)}) %all-to-all-start.2) | async-done | bytes 1048608 | tf_op jit(solution)/shard_map/all_to_all | solution.py:255
  373.8 2.0 fusion.27
  (39 shorter events, 0.3 us)
Async XLA Ops:
  7.2 24.6 %copy-start = (bf16[2,1024,576]{1,2,0:T(8,128)(2,1)S(1)}, bf16[2,1024,576]{1,2,0:T(8,128)(2,1)}, u32[]{:S(2)}) copy-start(bf16[2,1024,576]{1,2,0:T(8,128)(2,1)} %param.21) | copy-start | bytes 7077892
  7.2 19.1 %copy-start.8 = (f32[512]{0:T(512)S(1)}, f32[512]{0:T(512)}, u32[]{:S(2)}) copy-start(f32[512]{0:T(512)} %param.26) | copy-start | bytes 6148
  7.2 21.1 %copy-start.3 = (bf16[512,512]{1,0:T(8,128)(2,1)S(1)}, bf16[512,512]{1,0:T(8,128)(2,1)}, u32[]{:S(2)}) copy-start(bf16[512,512]{1,0:T(8,128)(2,1)} %param.27) | copy-start | bytes 1572868
  7.2 21.1 %copy-start.5 = (bf16[128,512]{1,0:T(8,128)(2,1)S(1)}, bf16[128,512]{1,0:T(8,128)(2,1)}, u32[]{:S(2)}) copy-start(bf16[128,512]{1,0:T(8,128)(2,1)} %param.19) | copy-start | bytes 393220
  7.2 70.9 %reduce-scatter.2.cloned.1.call-start = ((), (), s32[]{:S(2)}) async-start(), calls=%async_computation.4 | async-start | bytes 1310720 | tf_op jit(solution)/shard_map/reduce_scatter | solution.py:225
  28.3 1.8 copy-start.6
  31.7 2.3 copy-start.2
  36.1 1.1 copy-start.4
  38.8 3.2 copy-start.7
  38.8 39.3 %copy-start.1 = (bf16[128,2048]{1,0:T(8,128)(2,1)S(1)}, bf16[128,2048]{1,0:T(8,128)(2,1)}, u32[]{:S(2)}) copy-start(bf16[128,2048]{1,0:T(8,128)(2,1)} %param.18) | copy-start | bytes 1572868
  42.0 170.2 %all-gather.3.cloned.1.call-start = ((), (), s32[]{:S(2)}) async-start(), calls=%async_computation.5 | async-start | bytes 5242880 | tf_op jit(solution)/shard_map/all_gather | solution.py:239
  331.2 14.0 %copy-start.10 = (s32[2]{0:T(128)S(1)}, s32[2]{0:T(128)}, u32[]{:S(2)}) copy-start(s32[2]{0:T(128)} %param.24) | copy-start | bytes 28
  331.2 14.6 %copy-start.9 = (bf16[128,6]{0,1:T(8,128)(2,1)S(1)}, bf16[128,6]{0,1:T(8,128)(2,1)}, u32[]{:S(2)}) copy-start(bf16[128,6]{0,1:T(8,128)(2,1)} %param.32) | copy-start | bytes 4612
  331.2 42.6 %all-to-all-start.2 = ((bf16[64,16,512]{2,1,0:T(8,128)(2,1)}), bf16[64,16,512]{2,1,0:T(8,128)(2,1)S(1)}, u32[]{:S(2)}, u32[]{:S(2)}) async-start(bf16[64,16,512]{2,1,0:T(8,128)(2,1)} %reduce_sum.85), calls=%async_computation.3 | async-start | bytes 2097152 | tf_op jit(solution)/shard_map/all_to_all | solution.py:255
Sparse Core Ops, SparseCore 0:
  42.1 35.9 reduce-scatter.1
  133.0 79.1 all-gather.2

commit v3 on v2

--- a/solution.py
+++ b/solution.py
@@ -231,31 +231,62 @@
     normed_quarter = (
         residual_quarter * lax.rsqrt(square_sum / D + epsilon) * gain_quarter
     ).astype(jnp.bfloat16)
+    parity = tp_index % 2
+    upper = tp_index // 2
+    across = [(t, t ^ 2) for t in range(tp_size)]
+    beside = [(t, t ^ 1) for t in range(tp_size)]
+    other_quarter = lax.ppermute(normed_quarter, "tp", across)
+    half_rows = jnp.where(
+        upper == 0,
+        jnp.stack([normed_quarter, other_quarter], 1),
+        jnp.stack([other_quarter, normed_quarter], 1),
+    ).reshape(tok_rows, 2 * quarter)
     outgoing = lax.dot_general(
-        pick_table, normed_quarter, (((0,), (0,)), ((), ())), preferred_element_type=jnp.float32
-    ).astype(jnp.bfloat16)
-    outgoing = outgoing.reshape(experts_all, capacity, quarter)
-    arrived = lax.all_to_all(outgoing, "req", split_axis=0, concat_axis=0, tiled=True)
-    row_set = lax.all_gather(arrived, "tp", axis=0, tiled=False)
-    gate_w = w_gate[0].reshape(tp_size, quarter, -1)
-    up_w = w_up[0].reshape(tp_size, quarter, -1)
-    gate_act = jnp.einsum("qscf,qfh->sch", row_set, gate_w, preferred_element_type=jnp.float32)
-    up_act = jnp.einsum("qscf,qfh->sch", row_set, up_w, preferred_element_type=jnp.float32)
+        pick_table, half_rows, (((0,), (0,)), ((), ())), preferred_element_type=jnp.float32
+    ).astype(jnp.bfloat16)
+    outgoing = outgoing.reshape(experts_all, capacity, 2, quarter)
+    own_rows = lax.all_to_all(outgoing, "req", split_axis=0, concat_axis=0, tiled=True)
+    partner_rows = lax.ppermute(own_rows, "tp", beside)
+    sources = own_rows.shape[0]
+    gate_w = w_gate[0].reshape(2, 2, quarter, -1)
+    up_w = w_up[0].reshape(2, 2, quarter, -1)
+    down_w = w_down[0].reshape(w_down.shape[1], 2, 2, quarter)
+
+    def half_of(weight, axis, which):
+        return lax.dynamic_index_in_dim(weight, which, axis=axis, keepdims=False)
+
+    gate_act = jnp.einsum(
+        "scjf,jfh->sch", own_rows, half_of(gate_w, 1, parity), preferred_element_type=jnp.float32
+    ) + jnp.einsum(
+        "scjf,jfh->sch", partner_rows, half_of(gate_w, 1, 1 - parity),
+        preferred_element_type=jnp.float32,
+    )
+    up_act = jnp.einsum(
+        "scjf,jfh->sch", own_rows, half_of(up_w, 1, parity), preferred_element_type=jnp.float32
+    ) + jnp.einsum(
+        "scjf,jfh->sch", partner_rows, half_of(up_w, 1, 1 - parity),
+        preferred_element_type=jnp.float32,
+    )
     expert_hidden = (jax.nn.silu(gate_act) * up_act).astype(jnp.bfloat16)
-    partial_value = jnp.einsum(
-        "sch,hqf->qscf",
-        expert_hidden,
-        w_down[0].reshape(w_down.shape[1], tp_size, quarter),
-        preferred_element_type=jnp.float32,
-    )
-    partial_parts = lax.all_to_all(
-        partial_value.astype(jnp.bfloat16), "tp", split_axis=0, concat_axis=0, tiled=True
-    )
-    expert_out = jnp.sum(partial_parts.astype(jnp.float32), 0).astype(jnp.bfloat16)
-    shares = lax.all_to_all(expert_out, "req", split_axis=0, concat_axis=0, tiled=True)
-    routed = jnp.dot(
-        weights, shares.reshape(experts_all * capacity, quarter), preferred_element_type=jnp.float32
-    )
+    own_value = jnp.einsum(
+        "sch,hjf->scjf", expert_hidden, half_of(down_w, 2, parity),
+        preferred_element_type=jnp.float32,
+    )
+    partner_value = jnp.einsum(
+        "sch,hjf->scjf", expert_hidden, half_of(down_w, 2, 1 - parity),
+        preferred_element_type=jnp.float32,
+    ).astype(jnp.bfloat16)
+    pair_value = (
+        own_value + lax.ppermute(partner_value, "tp", beside).astype(jnp.float32)
+    ).astype(jnp.bfloat16)
+    shares = lax.all_to_all(pair_value, "req", split_axis=0, concat_axis=0, tiled=True)
+    routed_half = jnp.dot(
+        weights, shares.reshape(experts_all * capacity, 2 * quarter),
+        preferred_element_type=jnp.float32,
+    ).reshape(tok_rows, 2, quarter)
+    keep = half_of(routed_half, 1, upper)
+    give = half_of(routed_half, 1, 1 - upper)
+    routed = keep + lax.ppermute(give, "tp", across)
     layer_out = (residual_quarter + routed).astype(jnp.bfloat16)
     return (layer_out, accepted_rows)
 

time: 385 us -> 361 us (0.938)
  blocking collectives: 161 us -> 87.9 us
  waiting for transfers between devices: 125 us -> 167 us
  local copies, waits for them, and re-layouts: 22.3 us -> 36.4 us
    all_to_all x1 -> x0, blocking collectives: 95.7 us -> none  [on_device(): lax.all_to_all(partial_value.astype(jnp.bfloat16), 'tp', split_axis=0, co...]
    ppermute x0 -> x4, waiting for transfers between devices: none -> 85.7 us  [the longest x1 46 us: on_device(): lax.ppermute(partner_value, 'tp', beside).astype(jnp.float32)]
    all_gather x1 -> x0, waiting for transfers between devices: 66.1 us -> none  [on_device(): row_set = lax.all_gather(arrived, 'tp', axis=0, tiled=False)]
    all_to_all x1, blocking collectives: 44.8 us -> 67 us  [on_device(): lax.all_to_all(outgoing, 'req', split_axis=0, concat_axis=0, tiled=True)]
    all_to_all x1, waiting for transfers between devices: 25.1 us -> 46.8 us  [on_device(): lax.all_to_all(pair_value, 'req', split_axis=0, concat_axis=0, tiled=True)]
    dynamic_slice x0 -> x2, local copies, waits for them, and re-layouts: none -> 9.24 us  [half_of(): return lax.dynamic_index_in_dim(weight, which, axis=axis, keepdims=False)]
    all_to_all x1, starting transfers between devices: 14 us -> 8.15 us  [on_device(): lax.all_to_all(pair_value, 'req', split_axis=0, concat_axis=0, tiled=True)]
    ppermute x0 -> x4, starting transfers between devices: none -> 5.83 us  [the longest x1 5.6 us: on_device(): routed = keep + lax.ppermute(give, 'tp', across)]
  transfers between devices with their start and end apart: 3 -> 6, of which waited for: 3 -> 6; matrix products, arithmetic and copies ran while one was open for 5% -> 8% of each run, Pallas kernels for 0% -> 0%
where the time goes in v3:
time: 361 us; the launch traced here: 360 us
  waiting for transfers between devices  167 us (46%)
  blocking collectives  87.9 us (24%)
  local copies, waits for them, and re-layouts  36.4 us (10%)
  matrix products  32.2 us (9%)
  between operations  14.6 us (4%)
  starting transfers between devices  14 us (4%)
  other arithmetic  8.31 us (2%)
    all_to_all x1, blocking collectives, on_device(): lax.all_to_all(outgoing, 'req', split_axis=0, concat_axis=0, tiled=True)  67 us
    all_to_all x1, waiting for transfers between devices, on_device(): lax.all_to_all(pair_value, 'req', split_axis=0, concat_axis=0, tiled=True)  46.8 us
    ppermute x1, waiting for transfers between devices, on_device(): lax.ppermute(partner_value, 'tp', beside).astype(jnp.float32)  46 us
    reduce_scatter x1, waiting for transfers between devices, on_device(): lax.psum_scatter(attention_parts, 'tp', scatter_dimension=0, tiled=True)  34.5 us
    ppermute x1, waiting for transfers between devices, on_device(): partner_rows = lax.ppermute(own_rows, 'tp', beside)  22.6 us
    all_gather x1, blocking collectives, on_device(): compressed = lax.all_gather(compressed_part, 'tp', axis=1, tiled=True)  13.4 us
    ppermute x1, waiting for transfers between devices, on_device(): routed = keep + lax.ppermute(give, 'tp', across)  11.5 us
    dynamic_slice x2, local copies, waits for them, and re-layouts, half_of(): return lax.dynamic_index_in_dim(weight, which, axis=axis, keepdims=False)  9.24 us
  transfers between devices with their start and end apart: 6, of which 6 were waited for; matrix products, arithmetic and copies ran while one was open for 8% of the time, Pallas kernels for 0%

profile of v3, /device:TPU:1, one launch (start us, length us, event | category | flops | bytes accessed | tf_op | source)
XLA Modules:
  0.0 360.4 jit_solution(228477834421191585)
XLA Ops:
  7.3 1.7 convolution_convert_fusion.5
  9.0 13.4 %all_gather.3 = bf16[128,576]{0,1:T(8,128)(2,1)S(1)} all-gather(bf16[128,144]{0,1:T(8,128)(2,1)S(1)} %convolution_convert_fusion.5), channel_id=1, replica_groups=mesh['req'=64,'tp'=4] {'tp'}, dimensions={1}, use_global_device_ids=true | all-gather | bytes 184320 | tf_op jit(solution)/shard_map/all_gather | solution.py:188
  22.5 0.7 convert_element_type.96
  23.2 0.7 iota_compare_fusion.12
  23.9 1.0 convolution_minimum_fusion.6
  24.9 0.2 convolution_minimum_fusion.5
  25.1 0.2 convolution_minimum_fusion.4
  25.3 0.2 convolution_minimum_fusion.3
  25.5 0.2 convolution_minimum_fusion.2
  25.7 0.2 convolution_minimum_fusion.1
  25.9 0.3 fusion.72
  26.6 0.8 copy.100
  27.5 0.7 copy.101
  28.3 0.3 fusion.16
  28.6 0.4 copy.95
  29.1 1.0 copy.96
  30.4 1.4 fusion.73
  31.8 2.2 fusion.6
  34.1 0.4 fusion.48
  34.4 0.6 fusion.7
  35.0 1.1 fusion.20
  36.1 0.2 fusion.23
  36.3 0.9 reshape.168
  37.3 0.2 copy.126
  37.5 1.4 convolution_convert_fusion.4
  38.9 1.5 fusion.12
  40.6 0.4 fusion.19
  41.2 0.8 dynamic_slice.34
  42.0 34.5 %reduce-scatter.2.cloned.1.call-done = f32[1,128,512]{2,1,0:T(8,128)} async-done(((f32[4,128,512]{2,1,0:T(8,128)}), f32[1,128,512]{2,1,0:T(8,128)}) %reduce-scatter.2.cloned.1.call-update) | async-done | bytes 262160 | tf_op jit(solution)/shard_map/reduce_scatter | solution.py:225
  76.5 1.1 multiply_reduce_fusion
  77.6 7.4 %psum.7 = f32[128,1]{0,1:T(1,128)S(1)} all-reduce(f32[128,1]{0,1:T(1,128)S(1)} %bitcast.169), channel_id=1, replica_groups=mesh['req'=64,'tp'=4] {'tp'}, use_global_device_ids=true, to_apply=%region_11.12 | all-reduce | flops 128 | bytes 1024 | tf_op jit(solution)/shard_map/psum | solution.py:229
  85.0 1.0 multiply_convert_fusion
  86.2 0.5 fusion
  86.6 5.6 %collective-permute-done = bf16[128,512]{1,0:T(8,128)(2,1)S(1)} collective-permute-done((bf16[128,512]{1,0:T(8,128)(2,1)S(1)}, bf16[128,512]{1,0:T(8,128)(2,1)S(1)}, u32[]{:S(2)}, u32[]{:S(2)}) %collective-permute-start) | collective-permute-done | bytes 131104 | tf_op jit(solution)/shard_map/ppermute | solution.py:238
  92.5 0.7 convolution_convert_fusion.1
  93.2 2.8 reshape.173
  96.0 2.2 copy.109
  98.2 67.0 %all_to_all.10 = bf16[64,16,2,512]{3,1,2,0:T(8,128)(2,1)} all-to-all(bf16[64,16,2,512]{3,1,2,0:T(8,128)(2,1)S(1)} %copy.109), channel_id=1, replica_groups=mesh['req'=64,'tp'=4] {'req'}, dimensions={0} | all-to-all | bytes 4194304 | tf_op jit(solution)/shard_map/all_to_all | solution.py:248
  165.2 1.1 reshape_squeeze.10
  166.3 4.7 %reshape_squeeze.9 = bf16[2,2,512,352]{2,1,0,3:T(2,128)(2,1)} reshape(bf16[1,2048,352]{1,2,0:T(8,128)(2,1)} %param.33) | data formatting | bytes 2883584 | tf_op jit(solution)/shard_map/reshape;squeeze | solution.py:251
  171.0 3.8 %reshape_squeeze.11 = bf16[352,2,2,512]{3,2,1,0:T(2,128)(2,1)S(1)} reshape(bf16[1,352,2048]{2,1,0:T(8,128)(2,1)} %param.35) | data formatting | bytes 2883584 | tf_op jit(solution)/shard_map/reshape;squeeze | solution.py:253
  174.8 3.0 constant_dynamic-slice_fusion.1
  177.8 6.3 %constant_dynamic-slice_fusion.2 = (bf16[2,1,512,352]{2,1,0,3:T(2,128)(2,1)S(1)}, bf16[2,1,512,352]{2,1,0,3:T(2,128)(2,1)S(1)}, bf16[2,1,512,352]{2,1,0,3:T(2,128)(2,1)S(1)}, bf16[2,1,512,352]{2,1,0,3:T(2,128)(2,1)S(1)}) fusion(bf16[2,2,512,352]{2,1,0,3:T(2,128)(2,1)S(1)} %reshape_squeeze.10, s32[]{:T(128)S(6)} %select_n.81, s32[]{:T(128)S(6)} %select_n.80, ...), kind=kLoop, calls=%fused_computation.115 | loop fusion | bytes 5767176 | tf_op jit(solution)/shard_map/jit(dynamic_index_in_dim)/dynamic_slice | solution.py:256
  184.1 2.9 fusion.29
  187.0 2.9 fusion.31
  189.8 22.6 %collective-permute-done.1 = bf16[64,16,2,512]{3,1,2,0:T(8,128)(2,1)} collective-permute-done((bf16[64,16,2,512]{3,1,2,0:T(8,128)(2,1)}, bf16[64,16,2,512]{3,1,2,0:T(8,128)(2,1)}, u32[]{:S(2)}, u32[]{:S(2)}) %collective-permute-start.1) | collective-permute-done | bytes 2097184 | tf_op jit(solution)/shard_map/ppermute | solution.py:249
  212.5 2.9 fusion.30
  215.3 3.1 fusion.15
  218.4 1.3 convolution_convert_fusion
  219.8 46.0 %collective-permute-done.2 = bf16[64,16,2,512]{3,1,2,0:T(8,128)(2,1)S(1)} collective-permute-done((bf16[64,16,2,512]{3,1,2,0:T(8,128)(2,1)S(1)}, bf16[64,16,2,512]{3,1,2,0:T(8,128)(2,1)S(1)}, u32[]{:S(2)}, u32[]{:S(2)}) %collective-permute-start.2) | collective-permute-done | bytes 2097184 | tf_op jit(solution)/shard_map/ppermute | solution.py:280
  265.8 2.6 add_convert_fusion
  268.5 8.2 %all-to-all-start.1 = ((bf16[64,16,2,512]{3,1,2,0:T(8,128)(2,1)}), bf16[64,16,2,512]{3,1,2,0:T(8,128)(2,1)S(1)}, u32[]{:S(2)}, u32[]{:S(2)}) async-start(bf16[64,16,2,512]{3,1,2,0:T(8,128)(2,1)} %add_convert_fusion), calls=%async_computation.2 | async-start | bytes 4194304 | tf_op jit(solution)/shard_map/all_to_all | solution.py:282
  276.7 0.6 gather_fusion
  277.2 1.1 fusion.9
  278.4 46.8 %all-to-all-done.1 = bf16[64,16,2,512]{3,1,2,0:T(8,128)(2,1)S(1)} async-done(((bf16[64,16,2,512]{3,1,2,0:T(8,128)(2,1)}), bf16[64,16,2,512]{3,1,2,0:T(8,128)(2,1)S(1)}, u32[]{:S(2)}, u32[]{:S(2)}) %all-to-all-start.1) | async-done | bytes 2097184 | tf_op jit(solution)/shard_map/all_to_all | solution.py:282
  325.2 2.2 copy.116
  327.3 0.6 copy.136
  327.9 2.6 copy.117
  330.5 2.6 fusion.40
  333.1 0.7 dynamic-slice_bitcast_fusion
  333.9 5.6 %collective-permute-start.3 = (f32[128,512]{1,0:T(8,128)}, f32[128,512]{1,0:T(8,128)}, u32[]{:S(2)}, u32[]{:S(2)}) collective-permute-start(f32[128,512]{1,0:T(8,128)} %dynamic-slice_bitcast_fusion), channel_id=1, source_target_pairs={{0,2},{1,3},{2,0},{3,1},{4,6},{5,7},{6,4},{7,5},{8,10},{9,11},{10,... | collective-permute-start | bytes 786440 | tf_op jit(solution)/shard_map/ppermute | solution.py:289
  339.5 0.8 convolution_convert_fusion.3
  340.4 11.5 %collective-permute-done.3 = f32[128,512]{1,0:T(8,128)} collective-permute-done((f32[128,512]{1,0:T(8,128)}, f32[128,512]{1,0:T(8,128)}, u32[]{:S(2)}, u32[]{:S(2)}) %collective-permute-start.3) | collective-permute-done | bytes 262176 | tf_op jit(solution)/shard_map/ppermute | solution.py:289
  351.9 1.7 fusion.39
  (67 shorter events, 2.2 us)
Async XLA Ops:
  7.2 24.6 %copy-start = (bf16[2,1024,576]{1,2,0:T(8,128)(2,1)S(1)}, bf16[2,1024,576]{1,2,0:T(8,128)(2,1)}, u32[]{:S(2)}) copy-start(bf16[2,1024,576]{1,2,0:T(8,128)(2,1)} %param.21) | copy-start | bytes 7077892
  7.2 19.1 %copy-start.13 = (f32[512]{0:T(512)S(1)}, f32[512]{0:T(512)}, u32[]{:S(2)}) copy-start(f32[512]{0:T(512)} %param.26) | copy-start | bytes 6148
  7.2 21.1 %copy-start.8 = (bf16[512,512]{1,0:T(8,128)(2,1)S(1)}, bf16[512,512]{1,0:T(8,128)(2,1)}, u32[]{:S(2)}) copy-start(bf16[512,512]{1,0:T(8,128)(2,1)} %param.27) | copy-start | bytes 1572868
  7.2 21.1 %copy-start.10 = (bf16[128,512]{1,0:T(8,128)(2,1)S(1)}, bf16[128,512]{1,0:T(8,128)(2,1)}, u32[]{:S(2)}) copy-start(bf16[128,512]{1,0:T(8,128)(2,1)} %param.19) | copy-start | bytes 393220
  7.2 69.3 %reduce-scatter.2.cloned.1.call-start = ((), (), s32[]{:S(2)}) async-start(), calls=%async_computation.3 | async-start | bytes 1310720 | tf_op jit(solution)/shard_map/reduce_scatter | solution.py:225
  28.3 1.8 copy-start.11
  31.8 2.3 copy-start.6
  36.1 1.2 copy-start.9
  36.3 2.5 copy-start.4
  38.8 1.5 copy-start.12
  38.9 37.7 %copy-start.5 = (bf16[128,2048]{1,0:T(8,128)(2,1)S(1)}, bf16[128,2048]{1,0:T(8,128)(2,1)}, u32[]{:S(2)}) copy-start(bf16[128,2048]{1,0:T(8,128)(2,1)} %param.18) | copy-start | bytes 1572868
  86.1 6.2 %collective-permute-start = (bf16[128,512]{1,0:T(8,128)(2,1)S(1)}, bf16[128,512]{1,0:T(8,128)(2,1)S(1)}, u32[]{:S(2)}, u32[]{:S(2)}) collective-permute-start(bf16[128,512]{1,0:T(8,128)(2,1)S(1)} %multiply_convert_fusion), channel_id=1, source_target_pairs={{0,2},{1,3},{2,0},{3,1},{4,6},{5,7},{6,4},{7,5},{8,10},{9,11},{10,... | collective-permute-start | bytes 393224 | tf_op jit(solution)/shard_map/ppermute | solution.py:238
  98.2 67.1 %copy-start.7 = (bf16[1,2048,352]{1,2,0:T(8,128)(2,1)S(1)}, bf16[1,2048,352]{1,2,0:T(8,128)(2,1)}, u32[]{:S(2)}) copy-start(bf16[1,2048,352]{1,2,0:T(8,128)(2,1)} %param.34) | copy-start | bytes 4325380
  165.2 47.2 %collective-permute-start.1 = (bf16[64,16,2,512]{3,1,2,0:T(8,128)(2,1)}, bf16[64,16,2,512]{3,1,2,0:T(8,128)(2,1)}, u32[]{:S(2)}, u32[]{:S(2)}) collective-permute-start(bf16[64,16,2,512]{3,1,2,0:T(8,128)(2,1)} %all_to_all.10), channel_id=1, source_target_pairs={{0,1},{1,0},{2,3},{3,2},{4,5},{5,4},{6,7},{7,6},{8,9},{9,8},{10,11... | collective-permute-start | bytes 6291464 | tf_op jit(solution)/shard_map/ppermute | solution.py:249
  174.8 3.0 copy-start.2
  219.7 46.1 %collective-permute-start.2 = (bf16[64,16,2,512]{3,1,2,0:T(8,128)(2,1)S(1)}, bf16[64,16,2,512]{3,1,2,0:T(8,128)(2,1)S(1)}, u32[]{:S(2)}, u32[]{:S(2)}) collective-permute-start(bf16[64,16,2,512]{3,1,2,0:T(8,128)(2,1)S(1)} %convolution_convert_fusion), channel_id=1, source_target_pairs={{0,1},{1,0},{2,3},{3,2},{4,5},{5,4},{6,7},{7,6},{8,9},{9,8},{10,11... | collective-permute-start | bytes 6291464 | tf_op jit(solution)/shard_map/ppermute | solution.py:280
  268.5 8.2 %copy-start.15 = (s32[2]{0:T(128)S(1)}, s32[2]{0:T(128)}, u32[]{:S(2)}) copy-start(s32[2]{0:T(128)} %param.24) | copy-start | bytes 28
  268.5 8.8 %copy-start.14 = (bf16[128,6]{0,1:T(8,128)(2,1)S(1)}, bf16[128,6]{0,1:T(8,128)(2,1)}, u32[]{:S(2)}) copy-start(bf16[128,6]{0,1:T(8,128)(2,1)} %param.32) | copy-start | bytes 4612
  268.5 56.7 %all-to-all-start.1 = ((bf16[64,16,2,512]{3,1,2,0:T(8,128)(2,1)}), bf16[64,16,2,512]{3,1,2,0:T(8,128)(2,1)S(1)}, u32[]{:S(2)}, u32[]{:S(2)}) async-start(bf16[64,16,2,512]{3,1,2,0:T(8,128)(2,1)} %add_convert_fusion), calls=%async_computation.2 | async-start | bytes 4194304 | tf_op jit(solution)/shard_map/all_to_all | solution.py:282
  330.5 21.4 %copy-start.3 = (f32[1,128,512]{2,1,0:T(8,128)S(1)}, f32[1,128,512]{2,1,0:T(8,128)}, u32[]{:S(2)}) copy-start(f32[1,128,512]{2,1,0:T(8,128)} %reduce-scatter.2.cloned.1.call-done) | copy-start | bytes 786436
  330.5 23.1 %copy-start.1 = (bf16[2,1024,576]{1,2,0:T(8,128)(2,1)S(1)}, bf16[2,1024,576]{1,2,0:T(8,128)(2,1)}, u32[]{:S(2)}) copy-start(bf16[2,1024,576]{1,2,0:T(8,128)(2,1)} %param.21) | copy-start | bytes 7077892
  333.9 18.0 %collective-permute-start.3 = (f32[128,512]{1,0:T(8,128)}, f32[128,512]{1,0:T(8,128)}, u32[]{:S(2)}, u32[]{:S(2)}) collective-permute-start(f32[128,512]{1,0:T(8,128)} %dynamic-slice_bitcast_fusion), channel_id=1, source_target_pairs={{0,2},{1,3},{2,0},{3,1},{4,6},{5,7},{6,4},{7,5},{8,10},{9,11},{10,... | collective-permute-start | bytes 786440 | tf_op jit(solution)/shard_map/ppermute | solution.py:289
Sparse Core Ops, SparseCore 0:
  40.5 35.9 reduce-scatter.1
